TPU v7x, 512 devices: a whole 4x8x8 slice. The times are simulated.
512 devices in a mesh: area: 128 (over z, y, core), blk: 4 (over x).
Axes of the slice: x: 4, y: 8, z: 8, core: 2. Of those that a mesh axis runs over, the one named last changes fastest.
Arguments:
- activity: float32 [1024, 4, 64, 128], P('area', 'blk'), may hold values from -8 to 8
- ext_input: bfloat16 [1024, 4, 64, 128], P('area', 'blk'), may hold values from -5 to 5
- weights: bfloat16 [384, 4, 128, 512], P('area', 'blk'), may hold values from -0.25 to 0.25
- slot_dst: int32 [384], P('area'), may hold values from 0 to 7
- slot_src: int32 [384], P('area'), may hold values from 0 to 1023, as said below
- slot_count: int32 [128], P('area'), may hold values from 3 to 3, as said below
- hebb_mask: int32 [384], P('area'), may hold values 0 or 1
Outputs:
- final_activity: float32 [1024, 4, 64, 128], P('area', 'blk')
- plasticity: bfloat16 [384, 4, 128, 512], P('area', 'blk')
Inputs may be any that keep to these rules, and one draw needn't show every extreme that they name: Index i of area holds area i // 4; sources lie in areas listed for it by a connectome over the areas that always lists the area itself, the areas beside it on both sides (counted round) and the opposite one. Slots 0, 1 and 2 of index i of area have their source sub-blocks held by indices (i - 1) mod 128, (i + 1) mod 128 and (i + 64) mod 128. Among the occupied slots of one index of area, at most 1 have source sub-blocks held by one index of area (slot_src // 8); some index of area reaches 1. `slot_count`: some index of area has all 3 slots occupied.
All inputs are finite; a program needn't handle non-finite values. No bound on the sum of `hebb_mask` on one device may be relied on, other than what follows from the above.
Results may differ from a plain program's by a relative error of at most 0.014.
Values may be sent and summed in bfloat16 or wider, within the bound.
No kernel may reach another device: no remote copies, remote signals or barrier semaphores. Data moves between devices by JAX's collectives and lax.ppermute only.
A program may use at most 64 MiB of HBM per device.

v0:
```python
import jax
import jax.numpy as jnp
from jax import lax
from jax.sharding import PartitionSpec as P

STEPS = 4
euler_step = 0.5


def request_rosters(src_rows, count_now, sub_dev, n_areas, link_cap):
    slot_cap = src_rows.shape[0]
    slot_ids = jnp.arange(slot_cap)
    occupied = slot_ids < count_now
    owner_idx = src_rows // sub_dev
    local_idx = src_rows % sub_dev
    earlier = (
        (owner_idx[:, None] == owner_idx[None, :])
        & occupied[None, :]
        & (slot_ids[None, :] < slot_ids[:, None])
    )
    link_idx = jnp.minimum(jnp.sum(earlier.astype(jnp.int32), axis=1), link_cap - 1)
    matches = (
        occupied[:, None, None]
        & (owner_idx[:, None, None] == jnp.arange(n_areas)[None, :, None])
        & (link_idx[:, None, None] == jnp.arange(link_cap)[None, None, :])
    )
    request_table = jnp.sum(jnp.where(matches, (local_idx + 1)[:, None, None], 0), axis=0)
    return (occupied, owner_idx, link_idx, request_table)


def body(activity, ext_input, weights, slot_dst, slot_src, slot_count, hebb_mask):
    n_areas = lax.axis_size("area")
    my_blk = lax.axis_index("blk")
    sub_dev = activity.shape[0]
    trials = activity.shape[2]
    quarter = activity.shape[3]
    slot_cap = slot_src.shape[0]
    sub_width = weights.shape[3]
    link_cap = (slot_cap + n_areas - 1) // n_areas
    occupied, owner_idx, link_idx, request_table = request_rosters(
        slot_src, slot_count[0], sub_dev, n_areas, link_cap
    )
    needed_rows = lax.all_to_all(request_table, "area", split_axis=0, concat_axis=0, tiled=True)
    is_valid = needed_rows > 0
    pick_idx = jnp.maximum(needed_rows - 1, 0)
    select = ((slot_dst[:, None] == jnp.arange(sub_dev)[None, :]) & occupied[:, None]).astype(
        jnp.float32
    )
    slot_weights = weights[:, 0]
    pre_list = []
    post_list = []
    full_act, full_ext = (
        lax.all_gather(activity.astype(jnp.bfloat16), "blk", axis=1, tiled=True).astype(
            activity.dtype
        ),
        lax.all_gather(
            ext_input.astype(jnp.float32).astype(jnp.bfloat16), "blk", axis=1, tiled=True
        ).astype(jnp.float32),
    )
    current = full_act.transpose(0, 2, 1, 3).reshape(sub_dev, trials, sub_width)
    drive_in = full_ext.transpose(0, 2, 1, 3).reshape(sub_dev, trials, sub_width)
    rate_full = jnp.tanh(current).astype(jnp.bfloat16)
    for step_idx in range(STEPS):
        rates_own = lax.dynamic_slice_in_dim(rate_full, my_blk * quarter, quarter, 2)
        outbound_rates = jnp.where(
            is_valid[:, :, None, None], rates_own[pick_idx], jnp.zeros((), jnp.bfloat16)
        )
        presynaptic_rates = lax.all_to_all(
            outbound_rates, "area", split_axis=0, concat_axis=0, tiled=True
        )[owner_idx, link_idx]
        input_contribution = jnp.einsum(
            "xvy,xye->xve", presynaptic_rates, slot_weights, preferred_element_type=jnp.float32
        )
        partial_value = jnp.einsum(
            "kd,kts->dts", select, input_contribution, precision=lax.Precision.HIGHEST
        )
        partial_value, presynaptic_rates = (partial_value, presynaptic_rates)
        summed = lax.psum(partial_value.astype(jnp.bfloat16), "blk").astype(jnp.float32)
        current = current + euler_step * (summed - current + drive_in)
        rate_full = jnp.tanh(current).astype(jnp.bfloat16)
        pre_list.append(presynaptic_rates)
        post_list.append(rate_full)
    final_state = lax.dynamic_slice_in_dim(current, my_blk * quarter, quarter, 2)[:, None]
    pre_all = jnp.stack(pre_list, axis=1).astype(jnp.float32)
    pre_centered = (pre_all - jnp.mean(pre_all, axis=2, keepdims=True)).astype(jnp.bfloat16)
    pre_centered = pre_centered.reshape(slot_cap, STEPS * trials, quarter)
    post_all = jnp.stack(post_list, axis=1).astype(jnp.float32)
    post_centered = (post_all - jnp.mean(post_all, axis=2, keepdims=True)).astype(jnp.bfloat16)
    post_slot = post_centered[slot_dst].reshape(slot_cap, STEPS * trials, sub_width)
    change = jnp.einsum("knq,kns->kqs", pre_centered, post_slot, preferred_element_type=jnp.float32)
    gate_on = (occupied & (hebb_mask == 1)).astype(jnp.float32)
    norm_scale = (STEPS * trials) ** (-0.5)
    plasticity = (change * gate_on[:, None, None] * norm_scale).astype(jnp.bfloat16)[:, None]
    return (final_state, plasticity)


def solution(mesh):
    in_specs = (
        P("area", "blk", None, None),
        P("area", "blk", None, None),
        P("area", "blk", None, None),
        P("area"),
        P("area"),
        P("area"),
        P("area"),
    )
    out_specs = (P("area", "blk", None, None), P("area", "blk", None, None))
    return jax.shard_map(body, mesh=mesh, in_specs=in_specs, out_specs=out_specs, check_vma=False)
```

profile of v0, /device:TPU:8, one launch (start us, length us, event | category | flops | bytes accessed | tf_op | source)
XLA Modules:
  0.0 565.2 jit_solution(8893313728588876898)
XLA Ops:
  7.9 0.7 fusion.35
  8.5 1.2 and_convert_fusion
  9.7 0.2 convert_reduce_fusion.2
  9.9 0.6 copy-done.13
  10.5 0.1 fusion.34
  10.6 0.7 copy.91
  11.3 17.4 %all-to-all-start = ((s32[128,1,1]{2,1,0:T(1,128)}), s32[128,1,1]{2,1,0:T(1,128)S(1)}, u32[]{:S(2)}, u32[]{:S(2)}) async-start(s32[128,1,1]{2,1,0:T(1,128)} %copy.91), calls=%async_computation | async-start | bytes 131072 | tf_op jit(solution)/shard_map/all_to_all | solution.py:43
  28.7 1.0 convert_element_type.74
  29.7 13.1 %all_gather.6 = bf16[8,4,64,128]{3,2,1,0:T(8,128)(2,1)S(1)} all-gather(bf16[8,1,64,128]{3,2,1,0:T(8,128)(2,1)S(1)} %convert_element_type.74), channel_id=1, replica_groups=mesh['area'=128,'blk'=4] {'blk'}, dimensions={1}, use_global_device_ids=true | all-gather | bytes 655360 | tf_op jit(solution)/shard_map/all_gather | solution.py:53
  42.8 0.1 convert_bitcast_fusion.1
  43.0 0.6 copy.153
  43.6 0.1 fusion.30
  43.7 2.4 maximum_reduce_fusion
  46.0 2.2 gather_fusion
  48.2 2.4 compare_reduce_fusion
  50.6 3.2 fusion.4
  53.7 13.7 %all-to-all-start.1 = ((bf16[128,1,64,128]{3,2,1,0:T(8,128)(2,1)}), bf16[128,1,64,128]{3,2,1,0:T(8,128)(2,1)S(1)}, u32[]{:S(2)}, u32[]{:S(2)}) async-start(bf16[128,1,64,128]{3,2,1,0:T(8,128)(2,1)} %fusion.4), calls=%async_computation.1 | async-start | bytes 4194304 | tf_op jit(solution)/shard_map/all_to_all | solution.py:68
  67.5 0.7 fusion.42
  68.2 0.7 fusion.32
  68.9 52.5 %all-to-all-done.1 = bf16[128,1,64,128]{3,2,1,0:T(8,128)(2,1)S(1)} async-done(((bf16[128,1,64,128]{3,2,1,0:T(8,128)(2,1)}), bf16[128,1,64,128]{3,2,1,0:T(8,128)(2,1)S(1)}, u32[]{:S(2)}, u32[]{:S(2)}) %all-to-all-start.1) | async-done | bytes 2097184 | tf_op jit(solution)/shard_map/all_to_all | solution.py:68
  121.5 1.2 gather_fusion.1
  122.7 1.0 fusion.28
  123.7 1.7 convolution_convert_fusion.3
  125.5 14.4 %all_gather.7 = bf16[8,4,64,128]{3,2,1,0:T(8,128)(2,1)S(1)} all-gather(bf16[8,1,64,128]{3,2,1,0:T(8,128)(2,1)S(1)} %copy-done.10), channel_id=1, replica_groups=mesh['area'=128,'blk'=4] {'blk'}, dimensions={1}, use_global_device_ids=true | all-gather | bytes 655360 | tf_op jit(solution)/shard_map/all_gather | solution.py:56
  139.8 0.1 convert_bitcast_fusion
  140.0 32.7 %all-reduce.5.cloned.1.call-done = bf16[8,64,512]{2,0,1:T(8,128)(2,1)} async-done(((bf16[8,64,512]{2,0,1:T(8,128)(2,1)}), bf16[8,64,512]{2,0,1:T(8,128)(2,1)}) %all-reduce.5.cloned.1.call-update) | async-done | bytes 524304 | tf_op jit(solution)/shard_map/psum | solution.py:78
  172.6 2.2 tanh_convert_fusion.3
  174.9 0.8 copy-done.4
  175.7 2.2 gather_fusion.2
  177.9 1.8 fusion.3
  179.7 68.1 %all_to_all.29 = bf16[128,1,64,128]{3,2,1,0:T(8,128)(2,1)} all-to-all(bf16[128,1,64,128]{3,2,1,0:T(8,128)(2,1)S(1)} %fusion.3), channel_id=1, replica_groups=mesh['area'=128,'blk'=4] {'area'}, dimensions={0} | all-to-all | bytes 4194304 | tf_op jit(solution)/shard_map/all_to_all | solution.py:68
  247.8 2.2 gather_fusion.3
  250.0 0.2 fusion.26
  250.2 1.7 convolution_convert_fusion.2
  252.0 46.3 %all-reduce.7.cloned.1.call-done = bf16[8,64,512]{2,0,1:T(8,128)(2,1)} async-done(((bf16[8,64,512]{2,0,1:T(8,128)(2,1)}), bf16[8,64,512]{2,0,1:T(8,128)(2,1)}) %all-reduce.7.cloned.1.call-update) | async-done | bytes 524304 | tf_op jit(solution)/shard_map/psum | solution.py:78
  298.3 2.3 tanh_convert_fusion.2
  300.6 0.8 copy-done.2
  301.4 2.2 gather_fusion.4
  303.6 1.8 fusion.2
  305.4 68.1 %all_to_all.30 = bf16[128,1,64,128]{3,2,1,0:T(8,128)(2,1)} all-to-all(bf16[128,1,64,128]{3,2,1,0:T(8,128)(2,1)S(1)} %fusion.2), channel_id=1, replica_groups=mesh['area'=128,'blk'=4] {'area'}, dimensions={0} | all-to-all | bytes 4194304 | tf_op jit(solution)/shard_map/all_to_all | solution.py:68
  373.5 2.2 gather_fusion.5
  375.6 0.2 fusion.24
  375.8 1.7 convolution_convert_fusion.1
  377.5 46.4 %all-reduce.9.cloned.1.call-done = bf16[8,64,512]{2,0,1:T(8,128)(2,1)} async-done(((bf16[8,64,512]{2,0,1:T(8,128)(2,1)}), bf16[8,64,512]{2,0,1:T(8,128)(2,1)}) %all-reduce.9.cloned.1.call-update) | async-done | bytes 524304 | tf_op jit(solution)/shard_map/psum | solution.py:78
  423.9 2.6 tanh_convert_fusion.1
  426.5 0.8 copy-done.6
  427.3 2.1 gather_fusion.6
  429.5 3.1 fusion.1
  432.6 15.0 %all-to-all-start.4 = ((bf16[128,1,64,128]{3,2,1,0:T(8,128)(2,1)}), bf16[128,1,64,128]{3,2,1,0:T(8,128)(2,1)}, u32[]{:S(2)}, u32[]{:S(2)}) async-start(bf16[128,1,64,128]{3,2,1,0:T(8,128)(2,1)} %fusion.1), calls=%async_computation.4 | async-start | bytes 4194304 | tf_op jit(solution)/shard_map/all_to_all | solution.py:68
  447.7 53.6 %all-to-all-done.4 = bf16[128,1,64,128]{3,2,1,0:T(8,128)(2,1)} async-done(((bf16[128,1,64,128]{3,2,1,0:T(8,128)(2,1)}), bf16[128,1,64,128]{3,2,1,0:T(8,128)(2,1)}, u32[]{:S(2)}, u32[]{:S(2)}) %all-to-all-start.4) | async-done | bytes 2097184 | tf_op jit(solution)/shard_map/all_to_all | solution.py:68
  501.2 2.2 gather_fusion.7
  503.4 0.2 fusion.22
  503.6 1.7 convolution_convert_fusion
  505.3 0.1 convert_reduce_fusion.1
  505.4 0.1 fusion.21
  505.4 0.7 copy.106
  506.1 45.5 %all-reduce.11.cloned.1.call-done = bf16[8,64,512]{2,0,1:T(8,128)(2,1)} async-done(((bf16[8,64,512]{2,0,1:T(8,128)(2,1)}), bf16[8,64,512]{2,0,1:T(8,128)(2,1)}) %all-reduce.11.cloned.1.call-update) | async-done | bytes 524304 | tf_op jit(solution)/shard_map/psum | solution.py:78
  551.7 3.0 fusion.16
  554.6 0.3 convert_reduce_fusion
  554.9 0.5 fusion
  555.5 0.7 copy.107
  556.2 0.8 copy.109
  557.0 0.6 gather_fusion.8
  557.6 1.1 fusion.7
  (49 shorter events, 0.5 us)
Async XLA Ops:
  7.2 115.5 %copy-start = (bf16[3,1,128,512]{3,2,1,0:T(8,128)(2,1)S(1)}, bf16[3,1,128,512]{3,2,1,0:T(8,128)(2,1)}, u32[]{:S(2)}) copy-start(bf16[3,1,128,512]{3,2,1,0:T(8,128)(2,1)} %param.9) | copy-start | bytes 1179652
  9.7 19.0 %copy-start.11 = (pred[3]{0:T(512)(128)(4,1)}, pred[3]{0:T(512)(128)(4,1)S(1)}, u32[]{:S(2)}) copy-start(pred[3]{0:T(512)(128)(4,1)S(1)} %get-tuple-element.19) | copy-start | bytes 13
  9.9 0.6 copy-start.13
  11.3 32.3 %all-to-all-start = ((s32[128,1,1]{2,1,0:T(1,128)}), s32[128,1,1]{2,1,0:T(1,128)S(1)}, u32[]{:S(2)}, u32[]{:S(2)}) async-start(s32[128,1,1]{2,1,0:T(1,128)} %copy.91), calls=%async_computation | async-start | bytes 131072 | tf_op jit(solution)/shard_map/all_to_all | solution.py:43
  53.7 67.8 %all-to-all-start.1 = ((bf16[128,1,64,128]{3,2,1,0:T(8,128)(2,1)}), bf16[128,1,64,128]{3,2,1,0:T(8,128)(2,1)S(1)}, u32[]{:S(2)}, u32[]{:S(2)}) async-start(bf16[128,1,64,128]{3,2,1,0:T(8,128)(2,1)} %fusion.4), calls=%async_computation.1 | async-start | bytes 4194304 | tf_op jit(solution)/shard_map/all_to_all | solution.py:68
  67.5 105.2 %all-reduce.5.cloned.1.call-start = ((), (), s32[]{:S(2)}) async-start(), calls=%async_computation.5 | async-start | bytes 1048576 | tf_op jit(solution)/shard_map/psum | solution.py:78
  122.7 2.8 copy-start.10
  125.4 172.9 %all-reduce.7.cloned.1.call-start = ((), (), s32[]{:S(2)}) async-start(), calls=%async_computation.6 | async-start | bytes 1048576 | tf_op jit(solution)/shard_map/psum | solution.py:78
  174.9 0.8 copy-start.4
  247.8 50.5 %copy-start.1 = (bf16[8,64,512]{2,0,1:T(8,128)(2,1)S(1)}, bf16[8,64,512]{2,0,1:T(8,128)(2,1)}, u32[]{:S(2)}) copy-start(bf16[8,64,512]{2,0,1:T(8,128)(2,1)} %all-reduce.5.cloned.1.call-done) | copy-start | bytes 1572868
  251.9 172.0 %all-reduce.9.cloned.1.call-start = ((), (), s32[]{:S(2)}) async-start(), calls=%async_computation.7 | async-start | bytes 1048576 | tf_op jit(solution)/shard_map/psum | solution.py:78
  300.6 0.8 copy-start.2
  426.5 0.8 copy-start.6
  432.6 15.0 %copy-start.14 = (s32[3]{0:T(128)S(1)}, s32[3]{0:T(128)}, u32[]{:S(2)}) copy-start(s32[3]{0:T(128)} %param.10) | copy-start | bytes 40
  432.6 68.6 %all-to-all-start.4 = ((bf16[128,1,64,128]{3,2,1,0:T(8,128)(2,1)}), bf16[128,1,64,128]{3,2,1,0:T(8,128)(2,1)}, u32[]{:S(2)}, u32[]{:S(2)}) async-start(bf16[128,1,64,128]{3,2,1,0:T(8,128)(2,1)} %fusion.1), calls=%async_computation.4 | async-start | bytes 4194304 | tf_op jit(solution)/shard_map/all_to_all | solution.py:68
  447.6 57.7 %copy-start.9 = (bf16[3,64,128]{2,1,0:T(8,128)(2,1)S(1)}, bf16[3,64,128]{2,1,0:T(8,128)(2,1)}, u32[]{:S(2)}) copy-start(bf16[3,64,128]{2,1,0:T(8,128)(2,1)} %gather_fusion.1) | copy-start | bytes 147460
  447.6 104.1 %all-reduce.11.cloned.1.call-start = ((), (), s32[]{:S(2)}) async-start(), calls=%async_computation.8 | async-start | bytes 1048576 | tf_op jit(solution)/shard_map/psum | solution.py:78
  551.7 3.0 copy-start.3
  551.7 3.0 copy-start.5
  551.7 3.0 copy-start.7
  556.2 1.4 copy-start.8
  556.2 1.4 copy-start.12
Sparse Core Ops, SparseCore 0:
  125.5 47.0 all-reduce.4
  252.0 46.2 all-reduce.6
  377.7 46.2 all-reduce.8
  505.4 46.2 all-reduce.10
where the time goes:
time: 566 us; the launch traced here: 565 us
  waiting for transfers between devices  277 us (49%)
  blocking collectives  164 us (29%)
  starting transfers between devices  46.2 us (8%)
  other arithmetic  30.4 us (5%)
  local copies, waits for them, and re-layouts  23.6 us (4%)
  between operations  14.9 us (3%)
  matrix products  9.37 us (2%)
    psum x4, waiting for transfers between devices, body(): lax.psum(partial_value.astype(jnp.bfloat16), 'blk').astype(jnp.float32)  171 us
    all_to_all x2, blocking collectives, body(): lax.all_to_all(outbound_rates, 'area', split_axis=0, concat_axis=0, tiled...  136 us
    all_to_all x2, waiting for transfers between devices, body(): lax.all_to_all(outbound_rates, 'area', split_axis=0, concat_axis=0, tiled...  106 us
    all_to_all x2, starting transfers between devices, body(): lax.all_to_all(outbound_rates, 'area', split_axis=0, concat_axis=0, tiled...  28.7 us
    all_to_all x1, starting transfers between devices, body(): lax.all_to_all(request_table, 'area', split_axis=0, concat_axis=0, tiled=...  17.4 us
    all_gather x1, blocking collectives, body(): lax.all_gather(ext_input.astype(jnp.float32).astype(jnp.bfloat16), 'blk',...  14.4 us
    all_gather x1, blocking collectives, body(): lax.all_gather(activity.astype(jnp.bfloat16), 'blk', axis=1, tiled=True)  13.1 us
  transfers between devices with their start and end apart: 7, of which 6 were waited for; matrix products, arithmetic and copies ran while one was open for 1% of the time, Pallas kernels for 0%

commit v1 on v0

--- a/solution.py
+++ b/solution.py
@@ -53,8 +53,16 @@
         lax.all_gather(activity.astype(jnp.bfloat16), "blk", axis=1, tiled=True).astype(
             activity.dtype
         ),
-        lax.all_gather(
-            ext_input.astype(jnp.float32).astype(jnp.bfloat16), "blk", axis=1, tiled=True
+        jnp.concatenate(
+            lax.all_to_all(
+                jnp.stack(
+                    [ext_input.astype(jnp.float32).astype(jnp.bfloat16)] * lax.axis_size("blk")
+                ),
+                "blk",
+                0,
+                0,
+            ),
+            axis=1,
         ).astype(jnp.float32),
     )
     current = full_act.transpose(0, 2, 1, 3).reshape(sub_dev, trials, sub_width)

time: 566 us -> 563 us (level)
    all_to_all x0 -> x1, blocking collectives: none -> 15.5 us  [body(): lax.all_to_all(jnp.stack([ext_input.astype(jnp.float32).astype(jnp.bfloat...]
    all_gather x1 -> x0, blocking collectives: 14.4 us -> none  [body(): lax.all_gather(ext_input.astype(jnp.float32).astype(jnp.bfloat16), 'blk',...]
where the time goes in v1:
time: 563 us; the launch traced here: 562 us
  waiting for transfers between devices  276 us (49%)
  blocking collectives  165 us (29%)
  starting transfers between devices  46.2 us (8%)
  other arithmetic  28.2 us (5%)
  local copies, waits for them, and re-layouts  22.9 us (4%)
  between operations  14.9 us (3%)
  matrix products  9.36 us (2%)
    psum x4, waiting for transfers between devices, body(): lax.psum(partial_value.astype(jnp.bfloat16), 'blk').astype(jnp.float32)  170 us
    all_to_all x2, blocking collectives, body(): lax.all_to_all(outbound_rates, 'area', split_axis=0, concat_axis=0, tiled...  136 us
    all_to_all x2, waiting for transfers between devices, body(): lax.all_to_all(outbound_rates, 'area', split_axis=0, concat_axis=0, tiled...  106 us
    all_to_all x2, starting transfers between devices, body(): lax.all_to_all(outbound_rates, 'area', split_axis=0, concat_axis=0, tiled...  28.5 us
    all_to_all x1, starting transfers between devices, body(): lax.all_to_all(request_table, 'area', split_axis=0, concat_axis=0, tiled=...  17.4 us
    all_to_all x1, blocking collectives, body(): lax.all_to_all(jnp.stack([ext_input.astype(jnp.float32).astype(jnp.bfloat...  15.5 us
    all_gather x1, blocking collectives, body(): lax.all_gather(activity.astype(jnp.bfloat16), 'blk', axis=1, tiled=True)  13.1 us
  transfers between devices with their start and end apart: 7, of which 6 were waited for; matrix products, arithmetic and copies ran while one was open for 1% of the time, Pallas kernels for 0%

profile of v1, /device:TPU:8, one launch (start us, length us, event | category | flops | bytes accessed | tf_op | source)
XLA Modules:
  0.0 562.4 jit_solution(10849964323612475022)
XLA Ops:
  7.9 0.7 fusion.35
  8.5 1.2 and_convert_fusion
  9.8 0.2 convert_reduce_fusion.2
  10.0 0.5 copy-done.11
  10.5 0.1 fusion.34
  10.6 0.7 copy.93
  11.3 17.4 %all-to-all-start = ((s32[128,1,1]{2,1,0:T(1,128)}), s32[128,1,1]{2,1,0:T(1,128)S(1)}, u32[]{:S(2)}, u32[]{:S(2)}) async-start(s32[128,1,1]{2,1,0:T(1,128)} %copy.93), calls=%async_computation | async-start | bytes 131072 | tf_op jit(solution)/shard_map/all_to_all | solution.py:43
  28.7 1.0 convert_element_type.80
  29.7 13.1 %all_gather.3 = bf16[8,4,64,128]{3,2,1,0:T(8,128)(2,1)S(1)} all-gather(bf16[8,1,64,128]{3,2,1,0:T(8,128)(2,1)S(1)} %convert_element_type.80), channel_id=1, replica_groups=mesh['area'=128,'blk'=4] {'blk'}, dimensions={1}, use_global_device_ids=true | all-gather | bytes 655360 | tf_op jit(solution)/shard_map/all_gather | solution.py:53
  42.8 0.1 convert_bitcast_fusion.1
  43.0 0.6 copy.156
  43.6 0.1 fusion.30
  43.7 2.4 maximum_reduce_fusion
  46.0 2.1 gather_fusion
  48.2 2.4 compare_reduce_fusion
  50.5 3.1 fusion.4
  53.7 13.7 %all-to-all-start.1 = ((bf16[128,1,64,128]{3,2,1,0:T(8,128)(2,1)}), bf16[128,1,64,128]{3,2,1,0:T(8,128)(2,1)S(1)}, u32[]{:S(2)}, u32[]{:S(2)}) async-start(bf16[128,1,64,128]{3,2,1,0:T(8,128)(2,1)} %fusion.4), calls=%async_computation.1 | async-start | bytes 4194304 | tf_op jit(solution)/shard_map/all_to_all | solution.py:76
  67.5 0.6 fusion.42
  68.1 0.7 fusion.32
  68.8 52.6 %all-to-all-done.1 = bf16[128,1,64,128]{3,2,1,0:T(8,128)(2,1)S(1)} async-done(((bf16[128,1,64,128]{3,2,1,0:T(8,128)(2,1)}), bf16[128,1,64,128]{3,2,1,0:T(8,128)(2,1)S(1)}, u32[]{:S(2)}, u32[]{:S(2)}) %all-to-all-start.1) | async-done | bytes 2097184 | tf_op jit(solution)/shard_map/all_to_all | solution.py:76
  121.4 1.2 gather_fusion.1
  122.6 1.0 fusion.28
  123.7 1.7 convolution_convert_fusion.3
  125.4 0.1 copy.97
  125.5 0.1 stack.37
  125.6 15.5 %all_to_all.34 = bf16[4,8,1,64,128]{4,1,3,2,0:T(8,128)(2,1)S(1)} all-to-all(bf16[4,8,1,64,128]{4,1,3,2,0:T(8,128)(2,1)S(1)} %stack.37), channel_id=1, replica_groups=mesh['area'=128,'blk'=4] {'blk'}, dimensions={0} | all-to-all | bytes 1048576 | tf_op jit(solution)/shard_map/all_to_all | solution.py:57
  141.1 31.5 %all-reduce.5.cloned.1.call-done = bf16[8,64,512]{2,0,1:T(8,128)(2,1)} async-done(((bf16[8,64,512]{2,0,1:T(8,128)(2,1)}), bf16[8,64,512]{2,0,1:T(8,128)(2,1)}) %all-reduce.5.cloned.1.call-update) | async-done | bytes 524304 | tf_op jit(solution)/shard_map/psum | solution.py:86
  172.7 1.7 tanh_convert_fusion.3
  174.4 2.1 gather_fusion.2
  176.6 1.8 fusion.3
  178.4 68.3 %all_to_all.35 = bf16[128,1,64,128]{3,2,1,0:T(8,128)(2,1)} all-to-all(bf16[128,1,64,128]{3,2,1,0:T(8,128)(2,1)S(1)} %fusion.3), channel_id=1, replica_groups=mesh['area'=128,'blk'=4] {'area'}, dimensions={0} | all-to-all | bytes 4194304 | tf_op jit(solution)/shard_map/all_to_all | solution.py:76
  246.7 2.2 gather_fusion.3
  248.9 0.2 fusion.26
  249.1 1.7 convolution_convert_fusion.2
  250.8 46.4 %all-reduce.7.cloned.1.call-done = bf16[8,64,512]{2,0,1:T(8,128)(2,1)} async-done(((bf16[8,64,512]{2,0,1:T(8,128)(2,1)}), bf16[8,64,512]{2,0,1:T(8,128)(2,1)}) %all-reduce.7.cloned.1.call-update) | async-done | bytes 524304 | tf_op jit(solution)/shard_map/psum | solution.py:86
  297.3 1.8 tanh_convert_fusion.2
  299.1 0.8 copy-done.4
  299.9 2.1 gather_fusion.4
  302.1 1.8 fusion.2
  303.9 68.1 %all_to_all.36 = bf16[128,1,64,128]{3,2,1,0:T(8,128)(2,1)} all-to-all(bf16[128,1,64,128]{3,2,1,0:T(8,128)(2,1)S(1)} %fusion.2), channel_id=1, replica_groups=mesh['area'=128,'blk'=4] {'area'}, dimensions={0} | all-to-all | bytes 4194304 | tf_op jit(solution)/shard_map/all_to_all | solution.py:76
  372.0 2.2 gather_fusion.5
  374.1 0.2 fusion.24
  374.3 1.7 convolution_convert_fusion.1
  376.0 46.4 %all-reduce.9.cloned.1.call-done = bf16[8,64,512]{2,0,1:T(8,128)(2,1)} async-done(((bf16[8,64,512]{2,0,1:T(8,128)(2,1)}), bf16[8,64,512]{2,0,1:T(8,128)(2,1)}) %all-reduce.9.cloned.1.call-update) | async-done | bytes 524304 | tf_op jit(solution)/shard_map/psum | solution.py:86
  422.4 2.0 tanh_convert_fusion.1
  424.4 0.8 copy-done.2
  425.3 2.1 gather_fusion.6
  427.4 3.1 fusion.1
  430.5 14.7 %all-to-all-start.5 = ((bf16[128,1,64,128]{3,2,1,0:T(8,128)(2,1)}), bf16[128,1,64,128]{3,2,1,0:T(8,128)(2,1)}, u32[]{:S(2)}, u32[]{:S(2)}) async-start(bf16[128,1,64,128]{3,2,1,0:T(8,128)(2,1)} %fusion.1), calls=%async_computation.5 | async-start | bytes 4194304 | tf_op jit(solution)/shard_map/all_to_all | solution.py:76
  445.3 0.3 all-reduce.11.cloned.1.call-start
  445.6 53.4 %all-to-all-done.5 = bf16[128,1,64,128]{3,2,1,0:T(8,128)(2,1)} async-done(((bf16[128,1,64,128]{3,2,1,0:T(8,128)(2,1)}), bf16[128,1,64,128]{3,2,1,0:T(8,128)(2,1)}, u32[]{:S(2)}, u32[]{:S(2)}) %all-to-all-start.5) | async-done | bytes 2097184 | tf_op jit(solution)/shard_map/all_to_all | solution.py:76
  499.0 2.2 gather_fusion.7
  501.1 0.2 fusion.22
  501.3 1.7 convolution_convert_fusion
  503.1 0.1 fusion.21
  503.2 0.7 copy.109
  503.8 45.5 %all-reduce.11.cloned.1.call-done = bf16[8,64,512]{2,0,1:T(8,128)(2,1)} async-done(((bf16[8,64,512]{2,0,1:T(8,128)(2,1)}), bf16[8,64,512]{2,0,1:T(8,128)(2,1)}) %all-reduce.11.cloned.1.call-update) | async-done | bytes 524304 | tf_op jit(solution)/shard_map/psum | solution.py:86
  549.4 2.5 fusion.16
  551.9 0.3 convert_reduce_fusion
  552.2 0.5 fusion
  552.7 0.7 copy.110
  553.5 0.8 copy.112
  554.2 0.6 gather_fusion.8
  554.8 1.1 fusion.7
  (46 shorter events, 0.5 us)
Async XLA Ops:
  7.2 115.5 %copy-start = (bf16[3,1,128,512]{3,2,1,0:T(8,128)(2,1)S(1)}, bf16[3,1,128,512]{3,2,1,0:T(8,128)(2,1)}, u32[]{:S(2)}) copy-start(bf16[3,1,128,512]{3,2,1,0:T(8,128)(2,1)} %param.9) | copy-start | bytes 1179652
  9.8 18.9 %copy-start.9 = (pred[3]{0:T(512)(128)(4,1)}, pred[3]{0:T(512)(128)(4,1)S(1)}, u32[]{:S(2)}) copy-start(pred[3]{0:T(512)(128)(4,1)S(1)} %get-tuple-element.19) | copy-start | bytes 13
  10.0 0.5 copy-start.11
  11.3 32.3 %all-to-all-start = ((s32[128,1,1]{2,1,0:T(1,128)}), s32[128,1,1]{2,1,0:T(1,128)S(1)}, u32[]{:S(2)}, u32[]{:S(2)}) async-start(s32[128,1,1]{2,1,0:T(1,128)} %copy.93), calls=%async_computation | async-start | bytes 131072 | tf_op jit(solution)/shard_map/all_to_all | solution.py:43
  53.7 67.8 %all-to-all-start.1 = ((bf16[128,1,64,128]{3,2,1,0:T(8,128)(2,1)}), bf16[128,1,64,128]{3,2,1,0:T(8,128)(2,1)S(1)}, u32[]{:S(2)}, u32[]{:S(2)}) async-start(bf16[128,1,64,128]{3,2,1,0:T(8,128)(2,1)} %fusion.4), calls=%async_computation.1 | async-start | bytes 4194304 | tf_op jit(solution)/shard_map/all_to_all | solution.py:76
  67.4 105.3 %all-reduce.5.cloned.1.call-start = ((), (), s32[]{:S(2)}) async-start(), calls=%async_computation.6 | async-start | bytes 1048576 | tf_op jit(solution)/shard_map/psum | solution.py:86
  122.6 2.8 copy-start.8
  125.4 171.9 %all-reduce.7.cloned.1.call-start = ((), (), s32[]{:S(2)}) async-start(), calls=%async_computation.7 | async-start | bytes 1048576 | tf_op jit(solution)/shard_map/psum | solution.py:86
  246.7 50.6 %copy-start.1 = (bf16[8,64,512]{2,0,1:T(8,128)(2,1)S(1)}, bf16[8,64,512]{2,0,1:T(8,128)(2,1)}, u32[]{:S(2)}) copy-start(bf16[8,64,512]{2,0,1:T(8,128)(2,1)} %all-reduce.5.cloned.1.call-done) | copy-start | bytes 1572868
  250.8 171.6 %all-reduce.9.cloned.1.call-start = ((), (), s32[]{:S(2)}) async-start(), calls=%async_computation.8 | async-start | bytes 1048576 | tf_op jit(solution)/shard_map/psum | solution.py:86
  299.1 0.8 copy-start.4
  424.4 0.8 copy-start.2
  430.5 15.0 %copy-start.12 = (s32[3]{0:T(128)S(1)}, s32[3]{0:T(128)}, u32[]{:S(2)}) copy-start(s32[3]{0:T(128)} %param.10) | copy-start | bytes 40
  430.5 68.4 %all-to-all-start.5 = ((bf16[128,1,64,128]{3,2,1,0:T(8,128)(2,1)}), bf16[128,1,64,128]{3,2,1,0:T(8,128)(2,1)}, u32[]{:S(2)}, u32[]{:S(2)}) async-start(bf16[128,1,64,128]{3,2,1,0:T(8,128)(2,1)} %fusion.1), calls=%async_computation.5 | async-start | bytes 4194304 | tf_op jit(solution)/shard_map/all_to_all | solution.py:76
  445.3 57.7 %copy-start.7 = (bf16[3,64,128]{2,1,0:T(8,128)(2,1)S(1)}, bf16[3,64,128]{2,1,0:T(8,128)(2,1)}, u32[]{:S(2)}) copy-start(bf16[3,64,128]{2,1,0:T(8,128)(2,1)} %gather_fusion.1) | copy-start | bytes 147460
  445.3 104.1 %all-reduce.11.cloned.1.call-start = ((), (), s32[]{:S(2)}) async-start(), calls=%async_computation.9 | async-start | bytes 1048576 | tf_op jit(solution)/shard_map/psum | solution.py:86
  549.4 2.5 copy-start.3
  549.4 2.5 copy-start.5
  553.4 1.4 copy-start.6
  553.4 1.4 copy-start.10
Sparse Core Ops, SparseCore 0:
  125.5 47.1 all-reduce.4
  250.9 46.3 all-reduce.6
  376.1 46.2 all-reduce.8
  503.1 46.2 all-reduce.10
